TPU v7x, 32 devices: a whole 2x2x4 slice. The times are simulated.
32 devices in a mesh: ens: 2 (over y), step: 8 (over z, x), rows: 2 (over core).
Axes of the slice: x: 2, y: 2, z: 4, core: 2. Of those that a mesh axis runs over, the one named last changes fastest.
Arguments:
- iterates: float32 [8, 8, 32, 512], P('step', 'ens', 'rows'), parts along dimension 1, may hold values from -6 to 6
- window_start: float32 [8, 32, 512], P('ens', 'rows'), parts along dimension 0, may hold values from -6 to 6
- coarse: bfloat16 [24, 32, 512], P('ens', 'rows'), parts along dimension 0, may hold values from -6 to 6
- step_levels: int32 [8, 2], P('step'), may hold values from 0 to 16, as said below
- level_embed: bfloat16 [17, 128], replicated, may hold values from -3 to 3
- lift_weight: bfloat16 [16, 128], replicated, may hold values from -1.5 to 1.5
- conv_first: bfloat16 [3, 3, 128, 128], replicated, may hold values from -0.1875 to 0.1875
- conv_second: bfloat16 [3, 3, 128, 128], replicated, may hold values from -0.1875 to 0.1875
- project_weight: bfloat16 [128, 384], replicated, may hold values from -0.5 to 0.5
- mix_weight: bfloat16 [128, 128], replicated, may hold values from -6 to 6
- output_weight: bfloat16 [128, 4], replicated, may hold values from -0.5 to 0.5
Outputs:
- trajectory: float32 [8, 8, 32, 512], P('step', 'ens', 'rows'), parts along dimension 1
- denoised: float32 [8, 8, 32, 512], P('step', 'ens', 'rows'), parts along dimension 1
There are 2 independent parts, one for each index of `ens`. A program takes and returns all parts, laid end to end along the dimension named above; an argument that names none is the same for every part. Nothing has to cross between parts.
Inputs may be any that keep to these rules, and one draw needn't show every extreme that they name: `step_levels`: row k gives the plan levels at which step k starts and ends: each step ends 1 or 3 levels after it starts (half of the steps each), each step starts where the one before it ends, the first starts at level 0 and the last ends at level 16.
All inputs are finite; a program needn't handle non-finite values.
Results may differ from a plain program's by a relative error of at most 0.0028.
Values may be sent and summed in bfloat16 or wider, within the bound.
No kernel may reach another device: no remote copies, remote signals or barrier semaphores. Data moves between devices by JAX's collectives and lax.ppermute only.
A program may use at most 64 MiB of HBM per device.

v0:
```python
import jax
import jax.numpy as jnp
from jax import lax
from jax.sharding import PartitionSpec as P

HEAD_DIM = 64
SIGMA_TOP = 8.0
SIGMA_END = 0.002


def from_behind(x, axis, by):
    devices = lax.axis_size(axis)
    pairs = [(i, i + by) for i in range(devices) if 0 <= i + by < devices]
    return lax.ppermute(x, axis, pairs)


def with_halo(x, sides, width):
    for axis, dim in sides:
        devices, length = (lax.axis_size(axis), x.shape[dim])
        up = [(i, (i + 1) % devices) for i in range(devices - 1)]
        down = [(j, i) for i, j in up]
        last = lax.slice_in_dim(x, length - width, length, axis=dim)
        leading = lax.slice_in_dim(x, 0, width, axis=dim)
        before = lax.ppermute(last, axis, up)
        after = lax.ppermute(leading, axis, down)
        x = jnp.concatenate([before, x, after], axis=dim)
    return x


def noise_level(levels, level_count):
    fraction = levels.astype(jnp.float32) / jnp.float32(level_count - 1)
    return SIGMA_TOP * jnp.exp(fraction * jnp.log(jnp.float32(SIGMA_END / SIGMA_TOP)))


def normalize(values):
    return values * lax.rsqrt(jnp.mean(values * values, axis=-1, keepdims=True) + 1e-06)


def silu_norm(values):
    return jax.nn.silu(normalize(values)).astype(jnp.bfloat16)


def feature_map(values):
    return jnp.where(values > 0, values + 1.0, jnp.exp(jnp.minimum(values, 0.0)))


def conv_band(padded, weight):
    band_rows = padded.shape[0] - 2
    band_width = padded.shape[1]
    col_padded = jnp.pad(padded, ((0, 0), (1, 1), (0, 0)))
    stacked = jnp.concatenate(
        [
            col_padded[:, 0:band_width],
            col_padded[:, 1 : band_width + 1],
            col_padded[:, 2 : band_width + 2],
        ],
        axis=-1,
    )
    folded = weight.reshape(3, 3 * weight.shape[2], weight.shape[3])
    result = jnp.zeros((band_rows, band_width, weight.shape[3]), jnp.float32)
    for row_shift in range(3):
        result = result + jnp.einsum(
            "rwk,kf->rwf",
            stacked[row_shift : row_shift + band_rows],
            folded[row_shift],
            preferred_element_type=jnp.float32,
        )
    return result


def local(
    iterates,
    window_start,
    coarse,
    step_levels,
    level_embed,
    lift_weight,
    conv_first,
    conv_second,
    project_weight,
    mix_weight,
    output_weight,
):
    level_count = 2 * lax.axis_size("step") + 1
    previous = from_behind(iterates, "step", 1)
    current = jnp.where(lax.axis_index("step") == 0, window_start, previous[0])
    levels = step_levels[0]
    sigmas = noise_level(levels, level_count)
    sigma_low = sigmas[0]
    sigma_high = sigmas[1]
    spread = sigma_low * sigma_low + 0.25
    scale_in = lax.rsqrt(spread)
    scale_skip = 0.25 / spread
    scale_out = 0.5 * sigma_low * lax.rsqrt(spread)
    inputs = jnp.concatenate([(scale_in * current).astype(jnp.bfloat16), coarse], axis=0)
    picker = (jnp.arange(level_count) == levels[0]).astype(jnp.bfloat16)[None]
    embed_row = jnp.dot(picker, level_embed, preferred_element_type=jnp.float32)[0]
    lifted = (
        jnp.einsum("crw,cf->rwf", inputs, lift_weight, preferred_element_type=jnp.float32)
        + embed_row
    ).astype(jnp.bfloat16)
    band_rows = lifted.shape[0]
    band_width = lifted.shape[1]
    feat_dim = lifted.shape[2]
    act_first = silu_norm(lifted.astype(jnp.float32))
    padded = with_halo(act_first, (("rows", 0),), 1)
    middle = conv_band(padded, conv_first)
    act_next = silu_norm(middle)
    padded_next = with_halo(act_next, (("rows", 0),), 1)
    hidden = lifted.astype(jnp.float32) + conv_band(padded_next, conv_second)
    head_count = feat_dim // HEAD_DIM
    pooled = (
        hidden.reshape(band_rows // 4, 4, band_width // 4, 4, feat_dim)
        .mean(axis=(1, 3))
        .reshape(-1, feat_dim)
    )
    tokens = normalize(pooled).astype(jnp.bfloat16)
    projected = jnp.dot(tokens, project_weight, preferred_element_type=jnp.float32)
    queries = feature_map(projected[:, :feat_dim]).reshape(-1, head_count, HEAD_DIM)
    key_feats = feature_map(projected[:, feat_dim : 2 * feat_dim]).astype(jnp.bfloat16)
    value_rows = projected[:, 2 * feat_dim :].astype(jnp.bfloat16)
    key_piece = lax.all_gather(key_feats, "rows", axis=0, tiled=True)
    value_piece = lax.all_gather(value_rows, "rows", axis=0, tiled=True)
    piece_rows = key_piece.shape[0]
    key_heads = key_piece.reshape(piece_rows, head_count, HEAD_DIM)
    value_heads = value_piece.reshape(piece_rows, head_count, HEAD_DIM)
    summary_part = jnp.einsum(
        "thd,the->hde", key_heads, value_heads, preferred_element_type=jnp.float32
    )
    totals_part = jnp.sum(key_heads.astype(jnp.float32), axis=0)
    numerator = jnp.einsum("thd,hde->the", queries, summary_part, precision=lax.Precision.HIGHEST)
    denominator = jnp.einsum("thd,hd->th", queries, totals_part, precision=lax.Precision.HIGHEST)
    context = (numerator / denominator[:, :, None]).reshape(-1, feat_dim).astype(jnp.bfloat16)
    mixed = jnp.dot(context, mix_weight, preferred_element_type=jnp.float32)
    mixed = jnp.broadcast_to(
        mixed.reshape(band_rows // 4, 1, band_width // 4, 1, feat_dim),
        (band_rows // 4, 4, band_width // 4, 4, feat_dim),
    ).reshape(band_rows, band_width, feat_dim)
    act_out = silu_norm(hidden + mixed)
    out_field = jnp.einsum(
        "rwf,fc->crw", act_out, output_weight, preferred_element_type=jnp.float32
    )
    denoised = scale_skip * current + scale_out * out_field
    drift_step = (sigma_high - sigma_low) * (current - denoised) / sigma_low
    flattened = drift_step.reshape(1, -1)
    columns = lax.all_to_all(flattened, "step", split_axis=1, concat_axis=0, tiled=True)
    running = jnp.cumsum(columns, axis=0)
    summed = lax.all_to_all(running, "step", split_axis=0, concat_axis=1, tiled=True).reshape(
        drift_step.shape
    )
    trajectory = window_start + summed
    return (trajectory[None], denoised[None])


def solution(mesh):
    return jax.shard_map(
        local,
        mesh=mesh,
        in_specs=(
            P("step", "ens", "rows", None),
            P("ens", "rows", None),
            P("ens", "rows", None),
            P("step", None),
            P(),
            P(),
            P(),
            P(),
            P(),
            P(),
            P(),
        ),
        out_specs=(P("step", "ens", "rows", None), P("step", "ens", "rows", None)),
        check_vma=False,
    )
```

profile of v0, /device:TPU:0, one launch (start us, length us, event | category | flops | bytes accessed | tf_op | source)
XLA Modules:
  0.0 91.7 jit_solution(10086689503256885799)
XLA Ops:
  0.6 0.0 copy-start
  0.6 1.0 %copy.32 = f32[1,4,16,512]{3,1,2,0:T(4,128)S(1)} copy(f32[1,4,16,512]{3,2,1,0:T(8,128)} %param.11) | data formatting | bytes 262144 | tf_op args[0]
  1.7 4.8 %collective-permute-start = (f32[1,4,16,512]{3,1,2,0:T(4,128)S(1)}, f32[1,4,16,512]{3,1,2,0:T(4,128)S(1)}, u32[]{:S(2)}, u32[]{:S(2)}) collective-permute-start(f32[1,4,16,512]{3,1,2,0:T(4,128)S(1)} %copy.32), channel_id=1, source_target_pairs={{0,2},{2,4},{4,6},{6,8},{8,10},{10,12},{12,14},{1,3},{3,5},{5,7},{... | collective-permute-start | bytes 393224 | tf_op jit(solution)/shard_map/ppermute | solution.py:14
  6.5 0.7 exponential_multiply_fusion
  7.2 0.6 fusion.42
  9.2 1.0 %copy.34 = bf16[12,16,512]{2,0,1:T(8,128)(2,1)S(1)} copy(bf16[12,16,512]{2,1,0:T(8,128)(2,1)} %param.13) | data formatting | bytes 393216 | tf_op args[2]
  12.2 1.5 %convolution_bitcast_fusion.1 = f32[128]{0:T(128)S(1)} fusion(bf16[17,128]{1,0:T(8,128)(2,1)} %param.15, s32[]{:T(128)} %bitcast.110), kind=kOutput, calls=%fused_computation.34 | convolution fusion | flops 4369 | bytes 4868 | tf_op jit(solution)/shard_map/dot_general | solution.py:97
  13.6 0.0 collective-permute-done
  13.6 1.0 %multiply_convert_fusion.7 = (bf16[4,16,512]{2,0,1:T(4,128)(2,1)S(1)}, f32[4,16,512]{2,0,1:T(4,128)S(1)}) fusion(f32[]{:T(128)S(6)} %rsqrt.37, f32[1,4,16,512]{3,1,2,0:T(4,128)S(1)} %collective-permute-done, f32[4,16,512]{2,1,0:T(8,128)} %param.12, pred[]{:T(512)S(6)} %eq.11), kind=kLoop, calls=%fused_computation.52 | loop fusion | flops 98304 | bytes 458757 | tf_op jit(solution)/shard_map/convert_element_type | solution.py:95
  14.7 0.0 copy-start.3
  14.7 2.6 %fusion.7 = (f32[16,512]{1,0:T(8,128)S(1)}, bf16[16,512,128]{2,1,0:T(8,128)(2,1)S(1)}) fusion(f32[128]{0:T(128)S(1)} %convolution_bitcast_fusion.1, bf16[16,128]{1,0:T(8,128)(2,1)} %param.16, bf16[12,16,512]{2,0,1:T(8,128)(2,1)S(1)} %copy.34, bf16[4,16,512]{2,0,1:T(4,128)(2,1)S(1)} %get-tuple-element.12), kind=kOutput, calls=%fused_computation.14 | convolution fusion | flops 39313408 | bytes 2396672 | tf_op jit(solution)/shard_map/crw,cf->rwf/dot_general | solution.py:99
  17.3 1.5 %fusion.6 = bf16[16,512,128]{2,1,0:T(8,128)(2,1)S(1)} fusion(bf16[16,512,128]{2,1,0:T(8,128)(2,1)S(1)} %get-tuple-element.35, f32[16,512]{1,0:T(8,128)S(1)} %add_rsqrt_fusion.2), kind=kLoop, calls=%fused_computation.13 | loop fusion | flops 7340032 | bytes 4227072 | tf_op jit(solution)/shard_map/convert_element_type | solution.py:40
  18.8 1.5 %collective-permute-start.1 = (bf16[1,512,128]{2,1,0:T(8,128)(2,1)S(1)}, bf16[1,512,128]{2,1,0:T(8,128)(2,1)S(1)}, u32[]{:S(2)}, u32[]{:S(2)}) collective-permute-start(bf16[1,512,128]{2,1,0:T(8,128)(2,1)S(1)} %get-tuple-element.20), channel_id=1, source_target_pairs={{0,1},{2,3},{4,5},{6,7},{8,9},{10,11},{12,13},{14,15},{16,17},{18,... | collective-permute-start | bytes 393224 | tf_op jit(solution)/shard_map/ppermute | solution.py:24
  20.3 1.3 %collective-permute-start.2 = (bf16[1,512,128]{2,1,0:T(8,128)(2,1)S(1)}, bf16[1,512,128]{2,1,0:T(8,128)(2,1)S(1)}, u32[]{:S(2)}, u32[]{:S(2)}) collective-permute-start(bf16[1,512,128]{2,1,0:T(8,128)(2,1)S(1)} %get-tuple-element.21), channel_id=1, source_target_pairs={{1,0},{3,2},{5,4},{7,6},{9,8},{11,10},{13,12},{15,14},{17,16},{19,... | collective-permute-start | bytes 393224 | tf_op jit(solution)/shard_map/ppermute | solution.py:25
  21.6 0.0 copy-done.3
  21.7 0.0 collective-permute-done.1
  21.7 1.9 %collective-permute-done.2 = bf16[1,512,128]{2,1,0:T(8,128)(2,1)S(1)} collective-permute-done((bf16[1,512,128]{2,1,0:T(8,128)(2,1)S(1)}, bf16[1,512,128]{2,1,0:T(8,128)(2,1)S(1)}, u32[]{:S(2)}, u32[]{:S(2)}) %collective-permute-start.2) | collective-permute-done | bytes 131104 | tf_op jit(solution)/shard_map/ppermute | solution.py:25
  23.6 1.4 %fusion.12 = bf16[18,514,128]{2,1,0:T(8,128)(2,1)S(1)} fusion(bf16[1,512,128]{2,1,0:T(8,128)(2,1)S(1)} %collective-permute-done.2, bf16[16,512,128]{2,1,0:T(8,128)(2,1)S(1)} %fusion.6, bf16[1,512,128]{2,1,0:T(8,128)(2,1)S(1)} %collective-permute-done.1), kind=kLoop, calls=%fused_computation.27 | loop fusion | flops 14211072 | bytes 4727808 | tf_op jit(solution)/shard_map/concatenate | solution.py:26
  25.0 1.4 %fusion.37 = (bf16[18,512,128]{2,1,0:T(8,128)(2,1)S(1)}, bf16[18,512,128]{2,1,0:T(8,128)(2,1)S(1)}) fusion(bf16[18,514,128]{2,1,0:T(8,128)(2,1)S(1)} %fusion.12), kind=kLoop, calls=%fused_computation.71 | loop fusion | bytes 9437184 | tf_op jit(solution)/shard_map/slice | solution.py:53
  26.5 1.1 %pad_maximum_fusion = bf16[18,512,384]{2,1,0:T(8,128)(2,1)S(1)} fusion(bf16[18,512,128]{2,1,0:T(8,128)(2,1)S(1)} %get-tuple-element.17, bf16[1,512,128]{2,1,0:T(8,128)(2,1)S(1)} %collective-permute-done.2, bf16[16,512,128]{2,1,0:T(8,128)(2,1)S(1)} %fusion.6, bf16[1,512,128]{2,1,0:T(8,128)(2,1)S(1)} %collective-permute-done.1, ...), kind=kLoop, calls=%fused_computation.2 | loop fusion | flops 35389440 | bytes 14155776 | tf_op jit(solution)/shard_map/concatenate | solution.py:51
  27.6 1.8 %fusion.46 = f32[16,512,128]{2,1,0:T(8,128)S(1)} fusion(bf16[18,512,384]{2,1,0:T(8,128)(2,1)S(1)} %pad_maximum_fusion, bf16[384,128,1]{1,0,2:T(8,128)(2,1)S(1)} %bitcast.106), kind=kOutput, calls=%fused_computation.80 | convolution fusion | flops 805306368 | bytes 11370496 | tf_op jit(solution)/shard_map/rwk,kf->rwf/dot_general | solution.py:62
  29.4 1.8 %fusion.47 = f32[16,512,128]{2,1,0:T(8,128)S(1)} fusion(bf16[18,512,384]{2,1,0:T(8,128)(2,1)S(1)} %pad_maximum_fusion, bf16[384,128,1]{1,0,2:T(8,128)(2,1)S(1)} %bitcast.104), kind=kOutput, calls=%fused_computation.81 | convolution fusion | flops 805306368 | bytes 11370496 | tf_op jit(solution)/shard_map/rwk,kf->rwf/dot_general | solution.py:62
  31.2 2.1 %multiply_reduce_fusion.1 = (f32[16,512]{1,0:T(8,128)S(1)}, f32[16,512,128]{2,1,0:T(8,128)S(1)}) fusion(bf16[18,512,384]{2,1,0:T(8,128)(2,1)S(1)} %pad_maximum_fusion, bf16[384,128,1]{1,0,2:T(8,128)(2,1)S(1)} %bitcast.102, f32[16,512,128]{2,1,0:T(8,128)S(1)} %fusion.46, f32[16,512,128]{2,1,0:T(8,128)S(1)} %fusion.47), kind=kOutput, calls=%fused_computation.18 | convolution fusion | flops 809492480 | bytes 19791872 | tf_op jit(solution)/shard_map/rwk,kf->rwf/dot_general | solution.py:62
  33.3 0.0 copy-start.4
  33.3 1.4 %multiply_convert_fusion.1 = bf16[16,512,128]{2,1,0:T(8,128)(2,1)S(1)} fusion(f32[16,512,128]{2,1,0:T(8,128)S(1)} %get-tuple-element.37, f32[16,512]{1,0:T(8,128)S(1)} %add_rsqrt_fusion.1), kind=kLoop, calls=%fused_computation.17 | loop fusion | flops 6291456 | bytes 6324224 | tf_op jit(solution)/shard_map/convert_element_type | solution.py:40
  34.8 2.1 %collective-permute-start.3 = (bf16[1,512,128]{2,1,0:T(8,128)(2,1)S(1)}, bf16[1,512,128]{2,1,0:T(8,128)(2,1)S(1)}, u32[]{:S(2)}, u32[]{:S(2)}) collective-permute-start(bf16[1,512,128]{2,1,0:T(8,128)(2,1)S(1)} %get-tuple-element.18), channel_id=1, source_target_pairs={{0,1},{2,3},{4,5},{6,7},{8,9},{10,11},{12,13},{14,15},{16,17},{18,... | collective-permute-start | bytes 393224 | tf_op jit(solution)/shard_map/ppermute | solution.py:24
  36.9 1.5 %collective-permute-start.4 = (bf16[1,512,128]{2,1,0:T(8,128)(2,1)S(1)}, bf16[1,512,128]{2,1,0:T(8,128)(2,1)S(1)}, u32[]{:S(2)}, u32[]{:S(2)}) collective-permute-start(bf16[1,512,128]{2,1,0:T(8,128)(2,1)S(1)} %get-tuple-element.19), channel_id=1, source_target_pairs={{1,0},{3,2},{5,4},{7,6},{9,8},{11,10},{13,12},{15,14},{17,16},{19,... | collective-permute-start | bytes 393224 | tf_op jit(solution)/shard_map/ppermute | solution.py:25
  38.4 0.0 collective-permute-done.3
  38.4 1.7 %collective-permute-done.4 = bf16[1,512,128]{2,1,0:T(8,128)(2,1)S(1)} collective-permute-done((bf16[1,512,128]{2,1,0:T(8,128)(2,1)S(1)}, bf16[1,512,128]{2,1,0:T(8,128)(2,1)S(1)}, u32[]{:S(2)}, u32[]{:S(2)}) %collective-permute-start.4) | collective-permute-done | bytes 131104 | tf_op jit(solution)/shard_map/ppermute | solution.py:25
  40.1 1.4 %select_maximum_fusion = bf16[18,514,128]{2,1,0:T(8,128)(2,1)S(1)} fusion(bf16[1,512,128]{2,1,0:T(8,128)(2,1)S(1)} %collective-permute-done.4, bf16[16,512,128]{2,1,0:T(8,128)(2,1)S(1)} %multiply_convert_fusion.1, bf16[1,512,128]{2,1,0:T(8,128)(2,1)S(1)} %collective-permute-done.3), kind=kLoop, calls=%fused_computation.21 | loop fusion | flops 14211072 | bytes 4727808 | tf_op jit(solution)/shard_map/concatenate | solution.py:26
  41.5 1.5 %fusion.36 = (bf16[18,512,128]{2,1,0:T(8,128)(2,1)S(1)}, bf16[18,512,128]{2,1,0:T(8,128)(2,1)S(1)}) fusion(bf16[18,514,128]{2,1,0:T(8,128)(2,1)S(1)} %select_maximum_fusion), kind=kLoop, calls=%fused_computation.70 | loop fusion | bytes 9437184 | tf_op jit(solution)/shard_map/slice | solution.py:53
  43.0 1.1 %pad_maximum_fusion.1 = bf16[18,512,384]{2,1,0:T(8,128)(2,1)S(1)} fusion(bf16[18,512,128]{2,1,0:T(8,128)(2,1)S(1)} %get-tuple-element.15, bf16[1,512,128]{2,1,0:T(8,128)(2,1)S(1)} %collective-permute-done.4, bf16[16,512,128]{2,1,0:T(8,128)(2,1)S(1)} %multiply_convert_fusion.1, bf16[1,512,128]{2,1,0:T(8,128)(2,1)S(1)} %collective-permute-done.3, ...), kind=kLoop, calls=%fused_computation.3 | loop fusion | flops 35389440 | bytes 14155776 | tf_op jit(solution)/shard_map/concatenate | solution.py:51
  44.2 1.8 %fusion.48 = f32[16,512,128]{2,1,0:T(8,128)S(1)} fusion(bf16[18,512,384]{2,1,0:T(8,128)(2,1)S(1)} %pad_maximum_fusion.1, bf16[384,128,1]{1,0,2:T(8,128)(2,1)S(1)} %bitcast.107), kind=kOutput, calls=%fused_computation.82 | convolution fusion | flops 805306368 | bytes 11370496 | tf_op jit(solution)/shard_map/rwk,kf->rwf/dot_general | solution.py:62
  46.0 1.8 %fusion.49 = f32[16,512,128]{2,1,0:T(8,128)S(1)} fusion(bf16[18,512,384]{2,1,0:T(8,128)(2,1)S(1)} %pad_maximum_fusion.1, bf16[384,128,1]{1,0,2:T(8,128)(2,1)S(1)} %bitcast.105), kind=kOutput, calls=%fused_computation.83 | convolution fusion | flops 805306368 | bytes 11370496 | tf_op jit(solution)/shard_map/rwk,kf->rwf/dot_general | solution.py:62
  47.8 3.9 %convert_add_fusion = f32[16,512,128]{2,1,0:T(8,128)} fusion(bf16[16,512,128]{2,1,0:T(8,128)(2,1)S(1)} %get-tuple-element.35, f32[16,512,128]{2,1,0:T(8,128)S(1)} %fusion.48, f32[16,512,128]{2,1,0:T(8,128)S(1)} %fusion.49, bf16[18,512,384]{2,1,0:T(8,128)(2,1)S(1)} %pad_maximum_fusion.1, bf16[384,128,1]{1,0,2:T(8,128)(2,1)S(1)} %bitcast.103), kind=kOutput, calls=%fused_computation.4 | convolution fusion | flops 809500672 | bytes 21856256 | tf_op jit(solution)/shard_map/rwk,kf->rwf/dot_general | solution.py:62
  51.7 3.2 %reduce_sum.60 = f32[4,128,128]{2,1,0:T(8,128)S(1)} reduce(f32[4,4,128,4,128]{4,3,2,1,0:T(4,128)} %bitcast.96, f32[]{:T(128)} %constant.40.clone.1), dimensions={1,3}, to_apply=%region_2.3 | reduce | flops 983040 | bytes 4456452 | tf_op jit(solution)/shard_map/reduce_sum | solution.py:114
  54.9 0.1 multiply_reduce_fusion.2
  55.0 0.1 fusion.21
  55.2 0.3 fusion.43
  55.5 0.1 exponential_select_fusion
  55.7 2.0 %all_gather.6 = bf16[1024,128]{0,1:T(8,128)(2,1)S(1)} all-gather(bf16[512,128]{0,1:T(8,128)(2,1)S(1)} %get-tuple-element.23), channel_id=1, replica_groups=mesh['ens'=2,'step'=8,'rows'=2] {'rows'}, dimensions={0}, use_global_device_ids=true | all-gather | bytes 393216 | tf_op jit(solution)/shard_map/all_gather | solution.py:122
  57.6 0.1 convert_reduce_fusion
  57.8 0.1 reshape.147
  57.8 0.2 fusion.45
  58.1 2.2 %all_gather.7 = bf16[1024,128]{0,1:T(8,128)(2,1)S(1)} all-gather(bf16[512,128]{0,1:T(8,128)(2,1)S(1)} %slice.130), channel_id=1, replica_groups=mesh['ens'=2,'step'=8,'rows'=2] {'rows'}, dimensions={0}, use_global_device_ids=true | all-gather | bytes 393216 | tf_op jit(solution)/shard_map/all_gather | solution.py:123
  60.3 0.2 fusion.44
  60.6 0.4 fusion.15
  61.0 0.2 fusion.24
  61.2 0.8 broadcast_in_dim.6
  62.0 1.1 %copy-done.1 = f32[16,512,128]{2,1,0:T(8,128)S(1)} copy-done((f32[16,512,128]{2,1,0:T(8,128)S(1)}, f32[16,512,128]{2,1,0:T(8,128)}, u32[]{:S(2)}) %copy-start.1) | copy-done | bytes 4194328
  63.2 1.2 %multiply_reduce_fusion = (f32[16,512]{1,0:T(8,128)S(1)}, f32[16,512,128]{2,1,0:T(8,128)S(1)}) fusion(f32[16,512,128]{2,1,0:T(8,128)S(1)} %copy-done.1, f32[16,512,128]{2,1,0:T(8,128)S(1)} %bitcast.97), kind=kLoop, calls=%fused_computation.16 | loop fusion | flops 3137536 | bytes 12615680 | tf_op jit(solution)/shard_map/reduce_sum | solution.py:36
  64.3 0.0 copy-done.6
  64.4 0.0 copy-start.2
  64.4 1.9 %fusion.17 = f32[4,16,512]{2,0,1:T(4,128)S(1)} fusion(f32[16,512,128]{2,1,0:T(8,128)S(1)} %get-tuple-element.11, f32[16,512]{1,0:T(8,128)S(1)} %add_rsqrt_fusion, f32[]{:T(128)S(6)} %mul.111, bf16[128,4]{0,1:T(4,128)(2,1)S(1)} %copy-done.6), kind=kOutput, calls=%fused_computation.33 | convolution fusion | flops 14712832 | bytes 4359172 | tf_op jit(solution)/shard_map/rwf,fc->crw/dot_general | solution.py:140
  66.3 0.7 fusion.26
  67.0 0.1 all_to_all.21
  67.2 12.0 %all_to_all.24 = f32[1,8,4096]{2,0,1:T(1,128)S(1)} all-to-all(f32[1,8,4096]{2,0,1:T(1,128)S(1)} %all_to_all.21), channel_id=1, replica_groups=mesh['ens'=2,'step'=8,'rows'=2] {'step'}, dimensions={1} | all-to-all | bytes 262144 | tf_op jit(solution)/shard_map/all_to_all | solution.py:146
  79.2 0.7 fusion.22
  80.0 3.4 %all-to-all-start.1 = ((f32[8,1,4096]{2,1,0:T(1,128)}), f32[8,1,4096]{2,1,0:T(1,128)S(1)}, u32[]{:S(2)}, u32[]{:S(2)}) async-start(f32[8,1,4096]{2,1,0:T(1,128)} %fusion.22), calls=%async_computation.1 | async-start | bytes 262144 | tf_op jit(solution)/shard_map/all_to_all | solution.py:148
  83.4 0.7 copy.39
  84.0 6.6 %all-to-all-done.1 = f32[8,1,4096]{2,1,0:T(1,128)S(1)} async-done(((f32[8,1,4096]{2,1,0:T(1,128)}), f32[8,1,4096]{2,1,0:T(1,128)S(1)}, u32[]{:S(2)}, u32[]{:S(2)}) %all-to-all-start.1) | async-done | bytes 131104 | tf_op jit(solution)/shard_map/all_to_all | solution.py:148
  90.6 0.3 reduce.2
  91.0 0.0 copy-done.2
  91.0 0.7 add_bitcast_fusion
  (19 shorter events, 0.3 us)
Async XLA Ops:
  0.6 54.6 %copy-start = (bf16[128,384]{1,0:T(8,128)(2,1)S(1)}, bf16[128,384]{1,0:T(8,128)(2,1)}, u32[]{:S(2)}) copy-start(bf16[128,384]{1,0:T(8,128)(2,1)} %param.19) | copy-start | bytes 294916
  1.7 12.0 %collective-permute-start = (f32[1,4,16,512]{3,1,2,0:T(4,128)S(1)}, f32[1,4,16,512]{3,1,2,0:T(4,128)S(1)}, u32[]{:S(2)}, u32[]{:S(2)}) collective-permute-start(f32[1,4,16,512]{3,1,2,0:T(4,128)S(1)} %copy.32), channel_id=1, source_target_pairs={{0,2},{2,4},{4,6},{6,8},{8,10},{10,12},{12,14},{1,3},{3,5},{5,7},{... | collective-permute-start | bytes 393224 | tf_op jit(solution)/shard_map/ppermute | solution.py:14
  14.7 7.0 %copy-start.3 = (bf16[3,3,128,128]{3,2,1,0:T(8,128)(2,1)S(1)}, bf16[3,3,128,128]{3,2,1,0:T(8,128)(2,1)}, u32[]{:S(2)}) copy-start(bf16[3,3,128,128]{3,2,1,0:T(8,128)(2,1)} %param.17) | copy-start | bytes 884740
  18.8 2.8 %collective-permute-start.1 = (bf16[1,512,128]{2,1,0:T(8,128)(2,1)S(1)}, bf16[1,512,128]{2,1,0:T(8,128)(2,1)S(1)}, u32[]{:S(2)}, u32[]{:S(2)}) collective-permute-start(bf16[1,512,128]{2,1,0:T(8,128)(2,1)S(1)} %get-tuple-element.20), channel_id=1, source_target_pairs={{0,1},{2,3},{4,5},{6,7},{8,9},{10,11},{12,13},{14,15},{16,17},{18,... | collective-permute-start | bytes 393224 | tf_op jit(solution)/shard_map/ppermute | solution.py:24
  20.3 3.2 %collective-permute-start.2 = (bf16[1,512,128]{2,1,0:T(8,128)(2,1)S(1)}, bf16[1,512,128]{2,1,0:T(8,128)(2,1)S(1)}, u32[]{:S(2)}, u32[]{:S(2)}) collective-permute-start(bf16[1,512,128]{2,1,0:T(8,128)(2,1)S(1)} %get-tuple-element.21), channel_id=1, source_target_pairs={{1,0},{3,2},{5,4},{7,6},{9,8},{11,10},{13,12},{15,14},{17,16},{19,... | collective-permute-start | bytes 393224 | tf_op jit(solution)/shard_map/ppermute | solution.py:25
  33.3 5.1 %copy-start.4 = (bf16[3,3,128,128]{3,2,1,0:T(8,128)(2,1)S(1)}, bf16[3,3,128,128]{3,2,1,0:T(8,128)(2,1)}, u32[]{:S(2)}) copy-start(bf16[3,3,128,128]{3,2,1,0:T(8,128)(2,1)} %param.18) | copy-start | bytes 884740
  34.8 3.6 %collective-permute-start.3 = (bf16[1,512,128]{2,1,0:T(8,128)(2,1)S(1)}, bf16[1,512,128]{2,1,0:T(8,128)(2,1)S(1)}, u32[]{:S(2)}, u32[]{:S(2)}) collective-permute-start(bf16[1,512,128]{2,1,0:T(8,128)(2,1)S(1)} %get-tuple-element.18), channel_id=1, source_target_pairs={{0,1},{2,3},{4,5},{6,7},{8,9},{10,11},{12,13},{14,15},{16,17},{18,... | collective-permute-start | bytes 393224 | tf_op jit(solution)/shard_map/ppermute | solution.py:24
  36.9 3.2 %collective-permute-start.4 = (bf16[1,512,128]{2,1,0:T(8,128)(2,1)S(1)}, bf16[1,512,128]{2,1,0:T(8,128)(2,1)S(1)}, u32[]{:S(2)}, u32[]{:S(2)}) collective-permute-start(bf16[1,512,128]{2,1,0:T(8,128)(2,1)S(1)} %get-tuple-element.19), channel_id=1, source_target_pairs={{1,0},{3,2},{5,4},{7,6},{9,8},{11,10},{13,12},{15,14},{17,16},{19,... | collective-permute-start | bytes 393224 | tf_op jit(solution)/shard_map/ppermute | solution.py:25
  51.7 9.3 %copy-start.5 = (bf16[128,128]{1,0:T(8,128)(2,1)S(1)}, bf16[128,128]{1,0:T(8,128)(2,1)}, u32[]{:S(2)}) copy-start(bf16[128,128]{1,0:T(8,128)(2,1)} %param.20) | copy-start | bytes 98308
  61.0 2.2 %copy-start.1 = (f32[16,512,128]{2,1,0:T(8,128)S(1)}, f32[16,512,128]{2,1,0:T(8,128)}, u32[]{:S(2)}) copy-start(f32[16,512,128]{2,1,0:T(8,128)} %convert_add_fusion) | copy-start | bytes 12582916
  63.2 1.2 %copy-start.6 = (bf16[128,4]{0,1:T(4,128)(2,1)S(1)}, bf16[128,4]{0,1:T(4,128)(2,1)}, u32[]{:S(2)}) copy-start(bf16[128,4]{0,1:T(4,128)(2,1)} %param.21) | copy-start | bytes 3076
  64.4 26.6 %copy-start.2 = (f32[4,16,512]{2,1,0:T(8,128)S(1)}, f32[4,16,512]{2,1,0:T(8,128)}, u32[]{:S(2)}) copy-start(f32[4,16,512]{2,1,0:T(8,128)} %param.12) | copy-start | bytes 393220
  80.0 10.7 %all-to-all-start.1 = ((f32[8,1,4096]{2,1,0:T(1,128)}), f32[8,1,4096]{2,1,0:T(1,128)S(1)}, u32[]{:S(2)}, u32[]{:S(2)}) async-start(f32[8,1,4096]{2,1,0:T(1,128)} %fusion.22), calls=%async_computation.1 | async-start | bytes 262144 | tf_op jit(solution)/shard_map/all_to_all | solution.py:148
where the time goes:
time: 92.3 us; the launch traced here: 91.7 us
  matrix products  20.5 us (22%)
  other arithmetic  17.1 us (19%)
  blocking collectives  16.2 us (18%)
  starting transfers between devices  14.5 us (16%)
  waiting for transfers between devices  10.2 us (11%)
  local copies, waits for them, and re-layouts  8.69 us (9%)
  between operations  4.39 us (5%)
    dot_general x6, matrix products, conv_band(): jnp.einsum('rwk,kf->rwf', stacked[row_shift:row_shift + band_rows], folde...  13.1 us
    all_to_all x1, blocking collectives, local(): lax.all_to_all(flattened, 'step', split_axis=1, concat_axis=0, tiled=True)  12 us
    all_to_all x1, waiting for transfers between devices, local(): lax.all_to_all(running, 'step', split_axis=0, concat_axis=1, tiled=True)  6.58 us
    ppermute x1, starting transfers between devices, from_behind(): return lax.ppermute(x, axis, pairs)  4.85 us
    unnamed x17, local copies, waits for them, and re-layouts  3.94 us
    ppermute x2, waiting for transfers between devices, with_halo(): after = lax.ppermute(leading, axis, down)  3.6 us
    ppermute x2, starting transfers between devices, with_halo(): before = lax.ppermute(last, axis, up)  3.53 us
    all_to_all x1, starting transfers between devices, local(): lax.all_to_all(running, 'step', split_axis=0, concat_axis=1, tiled=True)  3.37 us
  transfers between devices with their start and end apart: 6, of which 3 were waited for; matrix products, arithmetic and copies ran while one was open for 5% of the time, Pallas kernels for 0%

commit v1 on v0

--- a/solution.py
+++ b/solution.py
@@ -119,7 +119,10 @@
     queries = feature_map(projected[:, :feat_dim]).reshape(-1, head_count, HEAD_DIM)
     key_feats = feature_map(projected[:, feat_dim : 2 * feat_dim]).astype(jnp.bfloat16)
     value_rows = projected[:, 2 * feat_dim :].astype(jnp.bfloat16)
-    key_piece = lax.all_gather(key_feats, "rows", axis=0, tiled=True)
+    devices_2 = lax.axis_size("rows")
+    parts = jnp.stack([key_feats for _ in range(devices_2)])
+    parts = lax.all_to_all(parts, "rows", split_axis=0, concat_axis=0)
+    key_piece = jnp.concatenate(parts, axis=0)
     value_piece = lax.all_gather(value_rows, "rows", axis=0, tiled=True)
     piece_rows = key_piece.shape[0]
     key_heads = key_piece.reshape(piece_rows, head_count, HEAD_DIM)

time: 92.3 us -> 94.8 us (1.027)
  blocking collectives: 16.2 us -> 18.2 us
    all_to_all x0 -> x1, blocking collectives: none -> 3.94 us  [local(): parts = lax.all_to_all(parts, 'rows', split_axis=0, concat_axis=0)]
    all_gather x1 -> x0, blocking collectives: 1.99 us -> none  [local(): key_piece = lax.all_gather(key_feats, 'rows', axis=0, tiled=True)]
where the time goes in v1:
time: 94.8 us; the launch traced here: 94.1 us
  matrix products  20.5 us (22%)
  blocking collectives  18.2 us (19%)
  other arithmetic  17.2 us (18%)
  starting transfers between devices  14.5 us (15%)
  waiting for transfers between devices  10.2 us (11%)
  local copies, waits for them, and re-layouts  9.14 us (10%)
  between operations  4.41 us (5%)
    dot_general x6, matrix products, conv_band(): jnp.einsum('rwk,kf->rwf', stacked[row_shift:row_shift + band_rows], folde...  13.2 us
    all_to_all x1, blocking collectives, local(): lax.all_to_all(flattened, 'step', split_axis=1, concat_axis=0, tiled=True)  12 us
    all_to_all x1, waiting for transfers between devices, local(): lax.all_to_all(running, 'step', split_axis=0, concat_axis=1, tiled=True)  6.58 us
    ppermute x1, starting transfers between devices, from_behind(): return lax.ppermute(x, axis, pairs)  4.85 us
    unnamed x17, local copies, waits for them, and re-layouts  3.95 us
    all_to_all x1, blocking collectives, local(): parts = lax.all_to_all(parts, 'rows', split_axis=0, concat_axis=0)  3.94 us
    ppermute x2, waiting for transfers between devices, with_halo(): after = lax.ppermute(leading, axis, down)  3.6 us
    ppermute x2, starting transfers between devices, with_halo(): before = lax.ppermute(last, axis, up)  3.53 us
  transfers between devices with their start and end apart: 6, of which 3 were waited for; matrix products, arithmetic and copies ran while one was open for 5% of the time, Pallas kernels for 0%

profile of v1, /device:TPU:0, one launch (start us, length us, event | category | flops | bytes accessed | tf_op | source)
XLA Modules:
  0.0 94.1 jit_solution(10377423351612835618)
XLA Ops:
  0.6 0.0 copy-start
  0.6 1.0 %copy.34 = f32[1,4,16,512]{3,1,2,0:T(4,128)S(1)} copy(f32[1,4,16,512]{3,2,1,0:T(8,128)} %param.11) | data formatting | bytes 262144 | tf_op args[0]
  1.7 4.8 %collective-permute-start = (f32[1,4,16,512]{3,1,2,0:T(4,128)S(1)}, f32[1,4,16,512]{3,1,2,0:T(4,128)S(1)}, u32[]{:S(2)}, u32[]{:S(2)}) collective-permute-start(f32[1,4,16,512]{3,1,2,0:T(4,128)S(1)} %copy.34), channel_id=1, source_target_pairs={{0,2},{2,4},{4,6},{6,8},{8,10},{10,12},{12,14},{1,3},{3,5},{5,7},{... | collective-permute-start | bytes 393224 | tf_op jit(solution)/shard_map/ppermute | solution.py:14
  6.5 0.7 exponential_multiply_fusion
  7.2 0.6 fusion.43
  9.2 1.0 %copy.36 = bf16[12,16,512]{2,0,1:T(8,128)(2,1)S(1)} copy(bf16[12,16,512]{2,1,0:T(8,128)(2,1)} %param.13) | data formatting | bytes 393216 | tf_op args[2]
  12.2 1.5 %convolution_bitcast_fusion.1 = f32[128]{0:T(128)S(1)} fusion(bf16[17,128]{1,0:T(8,128)(2,1)} %param.15, s32[]{:T(128)} %bitcast.112), kind=kOutput, calls=%fused_computation.34 | convolution fusion | flops 4369 | bytes 4868 | tf_op jit(solution)/shard_map/dot_general | solution.py:97
  13.6 0.0 collective-permute-done
  13.6 1.0 %multiply_convert_fusion.7 = (bf16[4,16,512]{2,0,1:T(4,128)(2,1)S(1)}, f32[4,16,512]{2,0,1:T(4,128)S(1)}) fusion(f32[]{:T(128)S(6)} %rsqrt.37, f32[1,4,16,512]{3,1,2,0:T(4,128)S(1)} %collective-permute-done, f32[4,16,512]{2,1,0:T(8,128)} %param.12, pred[]{:T(512)S(6)} %eq.11), kind=kLoop, calls=%fused_computation.54 | loop fusion | flops 98304 | bytes 458757 | tf_op jit(solution)/shard_map/convert_element_type | solution.py:95
  14.7 0.0 copy-start.3
  14.7 2.6 %fusion.7 = (f32[16,512]{1,0:T(8,128)S(1)}, bf16[16,512,128]{2,1,0:T(8,128)(2,1)S(1)}) fusion(f32[128]{0:T(128)S(1)} %convolution_bitcast_fusion.1, bf16[16,128]{1,0:T(8,128)(2,1)} %param.16, bf16[12,16,512]{2,0,1:T(8,128)(2,1)S(1)} %copy.36, bf16[4,16,512]{2,0,1:T(4,128)(2,1)S(1)} %get-tuple-element.12), kind=kOutput, calls=%fused_computation.14 | convolution fusion | flops 39313408 | bytes 2396672 | tf_op jit(solution)/shard_map/crw,cf->rwf/dot_general | solution.py:99
  17.3 1.5 %fusion.6 = bf16[16,512,128]{2,1,0:T(8,128)(2,1)S(1)} fusion(bf16[16,512,128]{2,1,0:T(8,128)(2,1)S(1)} %get-tuple-element.35, f32[16,512]{1,0:T(8,128)S(1)} %add_rsqrt_fusion.2), kind=kLoop, calls=%fused_computation.13 | loop fusion | flops 7340032 | bytes 4227072 | tf_op jit(solution)/shard_map/convert_element_type | solution.py:40
  18.8 1.5 %collective-permute-start.1 = (bf16[1,512,128]{2,1,0:T(8,128)(2,1)S(1)}, bf16[1,512,128]{2,1,0:T(8,128)(2,1)S(1)}, u32[]{:S(2)}, u32[]{:S(2)}) collective-permute-start(bf16[1,512,128]{2,1,0:T(8,128)(2,1)S(1)} %get-tuple-element.20), channel_id=1, source_target_pairs={{0,1},{2,3},{4,5},{6,7},{8,9},{10,11},{12,13},{14,15},{16,17},{18,... | collective-permute-start | bytes 393224 | tf_op jit(solution)/shard_map/ppermute | solution.py:24
  20.3 1.3 %collective-permute-start.2 = (bf16[1,512,128]{2,1,0:T(8,128)(2,1)S(1)}, bf16[1,512,128]{2,1,0:T(8,128)(2,1)S(1)}, u32[]{:S(2)}, u32[]{:S(2)}) collective-permute-start(bf16[1,512,128]{2,1,0:T(8,128)(2,1)S(1)} %get-tuple-element.21), channel_id=1, source_target_pairs={{1,0},{3,2},{5,4},{7,6},{9,8},{11,10},{13,12},{15,14},{17,16},{19,... | collective-permute-start | bytes 393224 | tf_op jit(solution)/shard_map/ppermute | solution.py:25
  21.7 0.0 collective-permute-done.1
  21.7 1.9 %collective-permute-done.2 = bf16[1,512,128]{2,1,0:T(8,128)(2,1)S(1)} collective-permute-done((bf16[1,512,128]{2,1,0:T(8,128)(2,1)S(1)}, bf16[1,512,128]{2,1,0:T(8,128)(2,1)S(1)}, u32[]{:S(2)}, u32[]{:S(2)}) %collective-permute-start.2) | collective-permute-done | bytes 131104 | tf_op jit(solution)/shard_map/ppermute | solution.py:25
  23.6 1.4 %fusion.12 = bf16[18,514,128]{2,1,0:T(8,128)(2,1)S(1)} fusion(bf16[1,512,128]{2,1,0:T(8,128)(2,1)S(1)} %collective-permute-done.2, bf16[16,512,128]{2,1,0:T(8,128)(2,1)S(1)} %fusion.6, bf16[1,512,128]{2,1,0:T(8,128)(2,1)S(1)} %collective-permute-done.1), kind=kLoop, calls=%fused_computation.27 | loop fusion | flops 14211072 | bytes 4727808 | tf_op jit(solution)/shard_map/concatenate | solution.py:26
  25.0 1.4 %fusion.38 = (bf16[18,512,128]{2,1,0:T(8,128)(2,1)S(1)}, bf16[18,512,128]{2,1,0:T(8,128)(2,1)S(1)}) fusion(bf16[18,514,128]{2,1,0:T(8,128)(2,1)S(1)} %fusion.12), kind=kLoop, calls=%fused_computation.73 | loop fusion | bytes 9437184 | tf_op jit(solution)/shard_map/slice | solution.py:53
  26.5 1.1 %pad_maximum_fusion = bf16[18,512,384]{2,1,0:T(8,128)(2,1)S(1)} fusion(bf16[18,512,128]{2,1,0:T(8,128)(2,1)S(1)} %get-tuple-element.17, bf16[1,512,128]{2,1,0:T(8,128)(2,1)S(1)} %collective-permute-done.2, bf16[16,512,128]{2,1,0:T(8,128)(2,1)S(1)} %fusion.6, bf16[1,512,128]{2,1,0:T(8,128)(2,1)S(1)} %collective-permute-done.1, ...), kind=kLoop, calls=%fused_computation.2 | loop fusion | flops 35389440 | bytes 14155776 | tf_op jit(solution)/shard_map/concatenate | solution.py:51
  27.6 1.8 %fusion.47 = f32[16,512,128]{2,1,0:T(8,128)S(1)} fusion(bf16[18,512,384]{2,1,0:T(8,128)(2,1)S(1)} %pad_maximum_fusion, bf16[384,128,1]{1,0,2:T(8,128)(2,1)S(1)} %bitcast.108), kind=kOutput, calls=%fused_computation.82 | convolution fusion | flops 805306368 | bytes 11370496 | tf_op jit(solution)/shard_map/rwk,kf->rwf/dot_general | solution.py:62
  29.4 1.8 %fusion.48 = f32[16,512,128]{2,1,0:T(8,128)S(1)} fusion(bf16[18,512,384]{2,1,0:T(8,128)(2,1)S(1)} %pad_maximum_fusion, bf16[384,128,1]{1,0,2:T(8,128)(2,1)S(1)} %bitcast.106), kind=kOutput, calls=%fused_computation.83 | convolution fusion | flops 805306368 | bytes 11370496 | tf_op jit(solution)/shard_map/rwk,kf->rwf/dot_general | solution.py:62
  31.2 2.1 %multiply_reduce_fusion.1 = (f32[16,512]{1,0:T(8,128)S(1)}, f32[16,512,128]{2,1,0:T(8,128)S(1)}) fusion(bf16[18,512,384]{2,1,0:T(8,128)(2,1)S(1)} %pad_maximum_fusion, bf16[384,128,1]{1,0,2:T(8,128)(2,1)S(1)} %bitcast.104, f32[16,512,128]{2,1,0:T(8,128)S(1)} %fusion.47, f32[16,512,128]{2,1,0:T(8,128)S(1)} %fusion.48), kind=kOutput, calls=%fused_computation.18 | convolution fusion | flops 809492480 | bytes 19791872 | tf_op jit(solution)/shard_map/rwk,kf->rwf/dot_general | solution.py:62
  33.3 0.0 copy-start.4
  33.3 1.4 %multiply_convert_fusion.1 = bf16[16,512,128]{2,1,0:T(8,128)(2,1)S(1)} fusion(f32[16,512,128]{2,1,0:T(8,128)S(1)} %get-tuple-element.37, f32[16,512]{1,0:T(8,128)S(1)} %add_rsqrt_fusion.1), kind=kLoop, calls=%fused_computation.17 | loop fusion | flops 6291456 | bytes 6324224 | tf_op jit(solution)/shard_map/convert_element_type | solution.py:40
  34.8 2.1 %collective-permute-start.3 = (bf16[1,512,128]{2,1,0:T(8,128)(2,1)S(1)}, bf16[1,512,128]{2,1,0:T(8,128)(2,1)S(1)}, u32[]{:S(2)}, u32[]{:S(2)}) collective-permute-start(bf16[1,512,128]{2,1,0:T(8,128)(2,1)S(1)} %get-tuple-element.18), channel_id=1, source_target_pairs={{0,1},{2,3},{4,5},{6,7},{8,9},{10,11},{12,13},{14,15},{16,17},{18,... | collective-permute-start | bytes 393224 | tf_op jit(solution)/shard_map/ppermute | solution.py:24
  36.9 1.5 %collective-permute-start.4 = (bf16[1,512,128]{2,1,0:T(8,128)(2,1)S(1)}, bf16[1,512,128]{2,1,0:T(8,128)(2,1)S(1)}, u32[]{:S(2)}, u32[]{:S(2)}) collective-permute-start(bf16[1,512,128]{2,1,0:T(8,128)(2,1)S(1)} %get-tuple-element.19), channel_id=1, source_target_pairs={{1,0},{3,2},{5,4},{7,6},{9,8},{11,10},{13,12},{15,14},{17,16},{19,... | collective-permute-start | bytes 393224 | tf_op jit(solution)/shard_map/ppermute | solution.py:25
  38.4 0.0 collective-permute-done.3
  38.4 1.7 %collective-permute-done.4 = bf16[1,512,128]{2,1,0:T(8,128)(2,1)S(1)} collective-permute-done((bf16[1,512,128]{2,1,0:T(8,128)(2,1)S(1)}, bf16[1,512,128]{2,1,0:T(8,128)(2,1)S(1)}, u32[]{:S(2)}, u32[]{:S(2)}) %collective-permute-start.4) | collective-permute-done | bytes 131104 | tf_op jit(solution)/shard_map/ppermute | solution.py:25
  40.1 1.4 %select_maximum_fusion = bf16[18,514,128]{2,1,0:T(8,128)(2,1)S(1)} fusion(bf16[1,512,128]{2,1,0:T(8,128)(2,1)S(1)} %collective-permute-done.4, bf16[16,512,128]{2,1,0:T(8,128)(2,1)S(1)} %multiply_convert_fusion.1, bf16[1,512,128]{2,1,0:T(8,128)(2,1)S(1)} %collective-permute-done.3), kind=kLoop, calls=%fused_computation.21 | loop fusion | flops 14211072 | bytes 4727808 | tf_op jit(solution)/shard_map/concatenate | solution.py:26
  41.6 1.5 %fusion.37 = (bf16[18,512,128]{2,1,0:T(8,128)(2,1)S(1)}, bf16[18,512,128]{2,1,0:T(8,128)(2,1)S(1)}) fusion(bf16[18,514,128]{2,1,0:T(8,128)(2,1)S(1)} %select_maximum_fusion), kind=kLoop, calls=%fused_computation.72 | loop fusion | bytes 9437184 | tf_op jit(solution)/shard_map/slice | solution.py:53
  43.0 1.1 %pad_maximum_fusion.1 = bf16[18,512,384]{2,1,0:T(8,128)(2,1)S(1)} fusion(bf16[18,512,128]{2,1,0:T(8,128)(2,1)S(1)} %get-tuple-element.15, bf16[1,512,128]{2,1,0:T(8,128)(2,1)S(1)} %collective-permute-done.4, bf16[16,512,128]{2,1,0:T(8,128)(2,1)S(1)} %multiply_convert_fusion.1, bf16[1,512,128]{2,1,0:T(8,128)(2,1)S(1)} %collective-permute-done.3, ...), kind=kLoop, calls=%fused_computation.3 | loop fusion | flops 35389440 | bytes 14155776 | tf_op jit(solution)/shard_map/concatenate | solution.py:51
  44.2 1.8 %fusion.49 = f32[16,512,128]{2,1,0:T(8,128)S(1)} fusion(bf16[18,512,384]{2,1,0:T(8,128)(2,1)S(1)} %pad_maximum_fusion.1, bf16[384,128,1]{1,0,2:T(8,128)(2,1)S(1)} %bitcast.109), kind=kOutput, calls=%fused_computation.84 | convolution fusion | flops 805306368 | bytes 11370496 | tf_op jit(solution)/shard_map/rwk,kf->rwf/dot_general | solution.py:62
  46.0 1.8 %fusion.50 = f32[16,512,128]{2,1,0:T(8,128)S(1)} fusion(bf16[18,512,384]{2,1,0:T(8,128)(2,1)S(1)} %pad_maximum_fusion.1, bf16[384,128,1]{1,0,2:T(8,128)(2,1)S(1)} %bitcast.107), kind=kOutput, calls=%fused_computation.85 | convolution fusion | flops 805306368 | bytes 11370496 | tf_op jit(solution)/shard_map/rwk,kf->rwf/dot_general | solution.py:62
  47.8 3.9 %convert_add_fusion = f32[16,512,128]{2,1,0:T(8,128)} fusion(bf16[16,512,128]{2,1,0:T(8,128)(2,1)S(1)} %get-tuple-element.35, f32[16,512,128]{2,1,0:T(8,128)S(1)} %fusion.49, f32[16,512,128]{2,1,0:T(8,128)S(1)} %fusion.50, bf16[18,512,384]{2,1,0:T(8,128)(2,1)S(1)} %pad_maximum_fusion.1, bf16[384,128,1]{1,0,2:T(8,128)(2,1)S(1)} %bitcast.105), kind=kOutput, calls=%fused_computation.4 | convolution fusion | flops 809500672 | bytes 21856256 | tf_op jit(solution)/shard_map/rwk,kf->rwf/dot_general | solution.py:62
  51.7 3.2 %reduce_sum.60 = f32[4,128,128]{2,1,0:T(8,128)S(1)} reduce(f32[4,4,128,4,128]{4,3,2,1,0:T(4,128)} %bitcast.99, f32[]{:T(128)} %constant.40.clone.1), dimensions={1,3}, to_apply=%region_2.3 | reduce | flops 983040 | bytes 4456452 | tf_op jit(solution)/shard_map/reduce_sum | solution.py:114
  54.9 0.0 copy-start.5
  54.9 0.1 multiply_reduce_fusion.2
  55.1 0.1 fusion.21
  55.2 0.3 fusion.44
  55.5 0.1 exponential_select_fusion
  55.7 3.9 %all_to_all.29 = bf16[2,512,128]{1,2,0:T(8,128)(2,1)S(1)} all-to-all(bf16[2,512,128]{1,2,0:T(8,128)(2,1)S(1)} %pad_maximum_fusion.2), channel_id=1, replica_groups=mesh['ens'=2,'step'=8,'rows'=2] {'rows'}, dimensions={0} | all-to-all | bytes 524288 | tf_op jit(solution)/shard_map/all_to_all | solution.py:124
  59.7 0.1 convert_reduce_fusion
  59.8 0.1 reshape.143
  59.9 0.2 fusion.46
  60.1 0.3 copy.37
  60.4 0.2 reshape_reshape.3
  60.6 2.2 %all_gather.3 = bf16[1024,128]{0,1:T(8,128)(2,1)S(1)} all-gather(bf16[512,128]{0,1:T(8,128)(2,1)S(1)} %slice.132), channel_id=1, replica_groups=mesh['ens'=2,'step'=8,'rows'=2] {'rows'}, dimensions={0}, use_global_device_ids=true | all-gather | bytes 393216 | tf_op jit(solution)/shard_map/all_gather | solution.py:126
  62.8 0.2 fusion.45
  63.0 0.4 fusion.15
  63.5 0.2 fusion.25
  63.7 0.8 broadcast_in_dim.6
  64.5 1.1 %copy-done.1 = f32[16,512,128]{2,1,0:T(8,128)S(1)} copy-done((f32[16,512,128]{2,1,0:T(8,128)S(1)}, f32[16,512,128]{2,1,0:T(8,128)}, u32[]{:S(2)}) %copy-start.1) | copy-done | bytes 4194328
  65.6 1.2 %multiply_reduce_fusion = (f32[16,512]{1,0:T(8,128)S(1)}, f32[16,512,128]{2,1,0:T(8,128)S(1)}) fusion(f32[16,512,128]{2,1,0:T(8,128)S(1)} %copy-done.1, f32[16,512,128]{2,1,0:T(8,128)S(1)} %bitcast.100), kind=kLoop, calls=%fused_computation.16 | loop fusion | flops 3137536 | bytes 12615680 | tf_op jit(solution)/shard_map/reduce_sum | solution.py:36
  66.8 0.0 copy-start.2
  66.8 1.9 %fusion.17 = f32[4,16,512]{2,0,1:T(4,128)S(1)} fusion(f32[16,512,128]{2,1,0:T(8,128)S(1)} %get-tuple-element.11, f32[16,512]{1,0:T(8,128)S(1)} %add_rsqrt_fusion, f32[]{:T(128)S(6)} %mul.111, bf16[128,4]{0,1:T(4,128)(2,1)S(1)} %copy-done.6), kind=kOutput, calls=%fused_computation.33 | convolution fusion | flops 14712832 | bytes 4359172 | tf_op jit(solution)/shard_map/rwf,fc->crw/dot_general | solution.py:143
  68.7 0.7 fusion.27
  69.5 0.1 all_to_all.25
  69.7 12.0 %all_to_all.30 = f32[1,8,4096]{2,0,1:T(1,128)S(1)} all-to-all(f32[1,8,4096]{2,0,1:T(1,128)S(1)} %all_to_all.25), channel_id=1, replica_groups=mesh['ens'=2,'step'=8,'rows'=2] {'step'}, dimensions={1} | all-to-all | bytes 262144 | tf_op jit(solution)/shard_map/all_to_all | solution.py:149
  81.7 0.7 fusion.23
  82.4 3.4 %all-to-all-start.2 = ((f32[8,1,4096]{2,1,0:T(1,128)}), f32[8,1,4096]{2,1,0:T(1,128)S(1)}, u32[]{:S(2)}, u32[]{:S(2)}) async-start(f32[8,1,4096]{2,1,0:T(1,128)} %fusion.23), calls=%async_computation.2 | async-start | bytes 262144 | tf_op jit(solution)/shard_map/all_to_all | solution.py:151
  85.8 0.7 copy.42
  86.5 6.6 %all-to-all-done.2 = f32[8,1,4096]{2,1,0:T(1,128)S(1)} async-done(((f32[8,1,4096]{2,1,0:T(1,128)}), f32[8,1,4096]{2,1,0:T(1,128)S(1)}, u32[]{:S(2)}, u32[]{:S(2)}) %all-to-all-start.2) | async-done | bytes 131104 | tf_op jit(solution)/shard_map/all_to_all | solution.py:151
  93.1 0.3 reduce.2
  93.4 0.7 add_bitcast_fusion
  (22 shorter events, 0.3 us)
Async XLA Ops:
  0.6 54.6 %copy-start = (bf16[128,384]{1,0:T(8,128)(2,1)S(1)}, bf16[128,384]{1,0:T(8,128)(2,1)}, u32[]{:S(2)}) copy-start(bf16[128,384]{1,0:T(8,128)(2,1)} %param.19) | copy-start | bytes 294916
  1.7 12.0 %collective-permute-start = (f32[1,4,16,512]{3,1,2,0:T(4,128)S(1)}, f32[1,4,16,512]{3,1,2,0:T(4,128)S(1)}, u32[]{:S(2)}, u32[]{:S(2)}) collective-permute-start(f32[1,4,16,512]{3,1,2,0:T(4,128)S(1)} %copy.34), channel_id=1, source_target_pairs={{0,2},{2,4},{4,6},{6,8},{8,10},{10,12},{12,14},{1,3},{3,5},{5,7},{... | collective-permute-start | bytes 393224 | tf_op jit(solution)/shard_map/ppermute | solution.py:14
  14.7 7.0 %copy-start.3 = (bf16[3,3,128,128]{3,2,1,0:T(8,128)(2,1)S(1)}, bf16[3,3,128,128]{3,2,1,0:T(8,128)(2,1)}, u32[]{:S(2)}) copy-start(bf16[3,3,128,128]{3,2,1,0:T(8,128)(2,1)} %param.17) | copy-start | bytes 884740
  18.8 2.8 %collective-permute-start.1 = (bf16[1,512,128]{2,1,0:T(8,128)(2,1)S(1)}, bf16[1,512,128]{2,1,0:T(8,128)(2,1)S(1)}, u32[]{:S(2)}, u32[]{:S(2)}) collective-permute-start(bf16[1,512,128]{2,1,0:T(8,128)(2,1)S(1)} %get-tuple-element.20), channel_id=1, source_target_pairs={{0,1},{2,3},{4,5},{6,7},{8,9},{10,11},{12,13},{14,15},{16,17},{18,... | collective-permute-start | bytes 393224 | tf_op jit(solution)/shard_map/ppermute | solution.py:24
  20.3 3.2 %collective-permute-start.2 = (bf16[1,512,128]{2,1,0:T(8,128)(2,1)S(1)}, bf16[1,512,128]{2,1,0:T(8,128)(2,1)S(1)}, u32[]{:S(2)}, u32[]{:S(2)}) collective-permute-start(bf16[1,512,128]{2,1,0:T(8,128)(2,1)S(1)} %get-tuple-element.21), channel_id=1, source_target_pairs={{1,0},{3,2},{5,4},{7,6},{9,8},{11,10},{13,12},{15,14},{17,16},{19,... | collective-permute-start | bytes 393224 | tf_op jit(solution)/shard_map/ppermute | solution.py:25
  33.3 5.1 %copy-start.4 = (bf16[3,3,128,128]{3,2,1,0:T(8,128)(2,1)S(1)}, bf16[3,3,128,128]{3,2,1,0:T(8,128)(2,1)}, u32[]{:S(2)}) copy-start(bf16[3,3,128,128]{3,2,1,0:T(8,128)(2,1)} %param.18) | copy-start | bytes 884740
  34.8 3.6 %collective-permute-start.3 = (bf16[1,512,128]{2,1,0:T(8,128)(2,1)S(1)}, bf16[1,512,128]{2,1,0:T(8,128)(2,1)S(1)}, u32[]{:S(2)}, u32[]{:S(2)}) collective-permute-start(bf16[1,512,128]{2,1,0:T(8,128)(2,1)S(1)} %get-tuple-element.18), channel_id=1, source_target_pairs={{0,1},{2,3},{4,5},{6,7},{8,9},{10,11},{12,13},{14,15},{16,17},{18,... | collective-permute-start | bytes 393224 | tf_op jit(solution)/shard_map/ppermute | solution.py:24
  36.9 3.2 %collective-permute-start.4 = (bf16[1,512,128]{2,1,0:T(8,128)(2,1)S(1)}, bf16[1,512,128]{2,1,0:T(8,128)(2,1)S(1)}, u32[]{:S(2)}, u32[]{:S(2)}) collective-permute-start(bf16[1,512,128]{2,1,0:T(8,128)(2,1)S(1)} %get-tuple-element.19), channel_id=1, source_target_pairs={{1,0},{3,2},{5,4},{7,6},{9,8},{11,10},{13,12},{15,14},{17,16},{19,... | collective-permute-start | bytes 393224 | tf_op jit(solution)/shard_map/ppermute | solution.py:25
  54.9 8.5 %copy-start.5 = (bf16[128,128]{1,0:T(8,128)(2,1)S(1)}, bf16[128,128]{1,0:T(8,128)(2,1)}, u32[]{:S(2)}) copy-start(bf16[128,128]{1,0:T(8,128)(2,1)} %param.20) | copy-start | bytes 98308
  63.4 2.2 %copy-start.1 = (f32[16,512,128]{2,1,0:T(8,128)S(1)}, f32[16,512,128]{2,1,0:T(8,128)}, u32[]{:S(2)}) copy-start(f32[16,512,128]{2,1,0:T(8,128)} %convert_add_fusion) | copy-start | bytes 12582916
  65.6 1.2 %copy-start.6 = (bf16[128,4]{0,1:T(4,128)(2,1)S(1)}, bf16[128,4]{0,1:T(4,128)(2,1)}, u32[]{:S(2)}) copy-start(bf16[128,4]{0,1:T(4,128)(2,1)} %param.21) | copy-start | bytes 3076
  66.8 26.6 %copy-start.2 = (f32[4,16,512]{2,1,0:T(8,128)S(1)}, f32[4,16,512]{2,1,0:T(8,128)}, u32[]{:S(2)}) copy-start(f32[4,16,512]{2,1,0:T(8,128)} %param.12) | copy-start | bytes 393220
  82.4 10.7 %all-to-all-start.2 = ((f32[8,1,4096]{2,1,0:T(1,128)}), f32[8,1,4096]{2,1,0:T(1,128)S(1)}, u32[]{:S(2)}, u32[]{:S(2)}) async-start(f32[8,1,4096]{2,1,0:T(1,128)} %fusion.23), calls=%async_computation.2 | async-start | bytes 262144 | tf_op jit(solution)/shard_map/all_to_all | solution.py:151
